TPU v7x, 128 devices: a whole 4x4x4 slice. The times are simulated.
128 devices in a mesh: group: 8 (over y_lo, x), head: 16 (over y_hi, z, core).
Axes of the slice: x: 4, y: 4 (y_hi: 2, y_lo: 2; y = y_hi * 2 + y_lo), z: 4, core: 2. Of those that a mesh axis runs over, the one named last changes fastest.
Arguments:
- symbol_lookup_table: bfloat16 [65536, 2048], P(None, 'head'), may hold values from -6 to 6
- joined_linear_maps: float32 [5, 2048, 2048], P(None, 'group', 'head'), may hold values from -0.125 to 0.125
- feedforward_lookup_map: float32 [2048, 7168], P('group', 'head'), may hold values from -0.125 to 0.125
- timeblend_result_map: float32 [2048, 2048], P('head', 'group'), may hold values from -0.125 to 0.125
- feedforward_content_map: float32 [7168, 2048], P('head', 'group'), may hold values from -0.0625 to 0.0625
- lag_blend_coefs: float32 [8, 2048], replicated, may hold values from 0 to 1
- blend_narrowing_map: bfloat16 [2048, 160], replicated, may hold values from -0.125 to 0.125
- blend_widening_maps: bfloat16 [5, 32, 2048], replicated, may hold values from -0.59765625 to 0.59765625
- fading_narrowing_map: bfloat16 [2048, 64], replicated, may hold values from -0.125 to 0.125
- fading_widening_map: bfloat16 [64, 2048], P(None, 'head'), as said below
- initial_fading_power: float32 [2048], P('head'), may hold values from -12 to -2.9
- present_symbol_extra: float32 [2048], P('head'), may hold values from -3 to 3
- attender_scaling_coefs: float32 [2048], P('head'), may hold values from 0.5 to 2
- active_cluster_sheets: int32 [8], replicated, may hold values from 2 to 4, as said below
- sheets_for_inquiry: int32 [7], replicated, may hold values from 2 to 7, as said below
- sheet_symbol_indices: int32 [24, 256], replicated, may hold values from 0 to 65535
Outputs:
- hidden_states: bfloat16 [8192, 2048], P('group', 'head')
- page_states: float32 [32, 32, 4096], P('group', 'head')
- shift_edges: float32 [32, 2, 2048], P('group', None, 'head')
Inputs may be any that keep to these rules, and one draw needn't show every extreme that they name: `active_cluster_sheets`: they sum to 24; the two groups at one end of the axis, the first two or the last two, hold 4 pages each. `sheets_for_inquiry`: they sum to 24; the first page of every group but group 0 continues a request; the first or the last request holds 7 pages. `fading_widening_map`: each entry lies within 2.5 / sqrt(64) of zero.
All inputs are finite; a program needn't handle non-finite values.
Results may differ from a plain program's by a relative error of at most 0.017.
Values may be sent and summed in bfloat16 or wider, within the bound.
No kernel may reach another device: no remote copies, remote signals or barrier semaphores. Data moves between devices by JAX's collectives and lax.ppermute only.
A program may use at most 192 MiB of HBM per device.

v0:
```python
import jax
import jax.numpy as jnp
from jax import lax
from jax.sharding import PartitionSpec as P

ATTENTION_DEPTH = 64
PAGE = 256
SLOTS = 4
BLOCK = 128
EXACT_ARITHMETIC = lax.Precision.HIGHEST
LAYER_EPS = 1e-05
GROUP_EPS = 0.00064


def passed_along(value, axis, steps):
    count = lax.axis_size(axis)
    initial, last = (max(0, -steps), min(count, count - steps))
    return lax.ppermute(value, axis, [(source, source + steps) for source in range(initial, last)])


def layer_norm(value_rows):
    value_rows = value_rows.astype(jnp.float32)
    centered = value_rows - jnp.mean(value_rows, axis=-1, keepdims=True)
    return centered * lax.rsqrt(jnp.mean(centered * centered, axis=-1, keepdims=True) + LAYER_EPS)


def mixed_inputs(current, previous, lag_blend_coefs, blend_narrowing_map, blend_widening_maps):
    delta_rows = previous - current
    seeded = (current + delta_rows * lag_blend_coefs[0]).astype(jnp.bfloat16)
    low_rank = jnp.tanh(
        jnp.dot(seeded, blend_narrowing_map, preferred_element_type=jnp.float32)
    ).astype(jnp.bfloat16)
    rank_width = blend_widening_maps.shape[1]
    result_lines = []
    for number in range(5):
        column_part = low_rank[:, number * rank_width : (number + 1) * rank_width]
        offset = jnp.dot(
            column_part, blend_widening_maps[number], preferred_element_type=jnp.float32
        )
        result_lines.append(
            (current + delta_rows * (lag_blend_coefs[number + 1] + offset)).astype(jnp.bfloat16)
        )
    return result_lines


def log_decay(mixed_decay, fading_narrowing_map, fading_widening_map, initial_fading_power):
    hidden_low = jnp.tanh(
        jnp.dot(mixed_decay, fading_narrowing_map, preferred_element_type=jnp.float32)
    ).astype(jnp.bfloat16)
    return -jnp.exp(
        initial_fading_power
        + jnp.dot(hidden_low, fading_widening_map, preferred_element_type=jnp.float32)
    )


def group_norm(value_rows):
    shaped = value_rows.reshape(value_rows.shape[0], -1, ATTENTION_DEPTH)
    centered = shaped - jnp.mean(shaped, axis=-1, keepdims=True)
    normed = centered * lax.rsqrt(jnp.mean(centered * centered, axis=-1, keepdims=True) + GROUP_EPS)
    return normed.reshape(value_rows.shape)


def per_device(
    symbol_lookup_table,
    joined_linear_maps,
    feedforward_lookup_map,
    timeblend_result_map,
    feedforward_content_map,
    lag_blend_coefs,
    blend_narrowing_map,
    blend_widening_maps,
    fading_narrowing_map,
    fading_widening_map,
    initial_fading_power,
    present_symbol_extra,
    attender_scaling_coefs,
    active_cluster_sheets,
    sheets_for_inquiry,
    sheet_symbol_indices,
):
    group_count = lax.axis_size("group")
    group_here = lax.axis_index("group")
    head_here = lax.axis_index("head")
    features_on_shard = present_symbol_extra.shape[0]
    attenders_on_shard = features_on_shard // ATTENTION_DEPTH
    slot_rows = SLOTS * PAGE
    full_width = lag_blend_coefs.shape[1]
    group_number = jnp.arange(group_count, dtype=jnp.int32)
    pick_group = group_number == group_here
    live_count = jnp.sum(jnp.where(pick_group, active_cluster_sheets, 0))
    group_first = jnp.cumsum(active_cluster_sheets) - active_cluster_sheets
    first_page = jnp.sum(jnp.where(pick_group, group_first, 0))
    slot_number = jnp.arange(SLOTS, dtype=jnp.int32)
    slot_live = slot_number < live_count
    request_first = jnp.cumsum(sheets_for_inquiry) - sheets_for_inquiry
    page_here = first_page + slot_number
    begins = jnp.any(page_here[:, None] == request_first[None, :], axis=1)
    continues = jnp.where(slot_live & jnp.logical_not(begins), 1.0, 0.0).astype(jnp.float32)
    safe_page = jnp.where(slot_live, page_here, 0)
    tokens_here = jnp.take(sheet_symbol_indices, safe_page, axis=0)
    before_token = jnp.take(sheet_symbol_indices[:, -1], jnp.maximum(safe_page - 1, 0))
    edge_pad = jnp.concatenate([before_token, jnp.zeros((8 - SLOTS,), before_token.dtype)])
    all_tokens = jnp.concatenate([tokens_here.reshape(-1), edge_pad])
    own_rows = jnp.take(symbol_lookup_table, all_tokens, axis=0)
    gathered_rows = lax.all_gather(own_rows, "head", axis=1, tiled=True)
    embedded = gathered_rows[:slot_rows]
    edge_rows = gathered_rows[slot_rows : slot_rows + SLOTS]
    map_count = joined_linear_maps.shape[0]
    first_pack = jnp.concatenate([joined_linear_maps, timeblend_result_map.T[None]], axis=0).astype(
        jnp.bfloat16
    )
    second_pack = jnp.stack([feedforward_lookup_map, feedforward_content_map.T], axis=0).astype(
        jnp.bfloat16
    )
    first_full = lax.all_gather(first_pack, "group", axis=1, tiled=True)
    second_full = lax.all_gather(second_pack, "group", axis=1, tiled=True)
    projections = first_full[:map_count]
    output_weight_t = first_full[map_count]
    key_weight = second_full[0]
    value_weight_t = second_full[1]
    current = layer_norm(embedded)
    edge_first = layer_norm(edge_rows) * continues[:, None]
    current_pages = current.reshape(SLOTS, PAGE, full_width)
    previous = jnp.concatenate([edge_first[:, None, :], current_pages[:, :-1, :]], axis=1).reshape(
        slot_rows, full_width
    )
    mixed_decay, mixed_key, mixed_value, mixed_query, mixed_gate = mixed_inputs(
        current, previous, lag_blend_coefs, blend_narrowing_map, blend_widening_maps
    )
    fading_multipliers = log_decay(
        mixed_decay, fading_narrowing_map, fading_widening_map, initial_fading_power
    )
    acceptance_lines = jnp.dot(mixed_query, projections[0], preferred_element_type=jnp.float32)
    present_lookups = jnp.dot(mixed_key, projections[1], preferred_element_type=jnp.float32)
    present_contents = jnp.dot(mixed_value, projections[2], preferred_element_type=jnp.float32)
    gate_raw = jnp.dot(mixed_gate, projections[3], preferred_element_type=jnp.float32)
    gating = jax.nn.silu(gate_raw)
    blocks = slot_rows // BLOCK
    per_page = PAGE // BLOCK

    def to_blocks(value_rows):
        return value_rows.reshape(blocks, BLOCK, attenders_on_shard, ATTENTION_DEPTH).transpose(
            0, 2, 1, 3
        )

    block_index = jnp.arange(blocks, dtype=jnp.int32)
    block_start = block_index % per_page == 0
    block_slot = block_index // per_page
    slot_keep = continues * (slot_number > 0)
    keep_state = jnp.where(block_start, jnp.take(slot_keep, block_slot), 1.0)
    keep_factor = jnp.where(block_start, jnp.take(continues, block_slot), 1.0)
    attender_extra = present_symbol_extra.reshape(attenders_on_shard, ATTENTION_DEPTH)
    strictly_lower = jnp.arange(BLOCK)[:, None] > jnp.arange(BLOCK)[None, :]
    askers_b = to_blocks(acceptance_lines)
    lookups_b = to_blocks(present_lookups)
    values_b = to_blocks(present_contents)
    decay_b = to_blocks(fading_multipliers)
    inclusive = jnp.cumsum(decay_b, axis=2)
    exclusive = inclusive - decay_b
    query_scaled = askers_b * jnp.exp(exclusive)
    key_scaled = lookups_b * jnp.exp(-inclusive)
    scores = jnp.einsum("bhts,bhus->bhtu", query_scaled, key_scaled, precision=EXACT_ARITHMETIC)
    scores = jnp.where(strictly_lower, scores, 0.0)
    selfpair_contribution = jnp.sum(askers_b * attender_extra[None, :, None, :] * lookups_b, axis=3)
    intra = (
        jnp.einsum("bhtu,bhuj->bhtj", scores, values_b, precision=EXACT_ARITHMETIC)
        + selfpair_contribution[..., None] * values_b
    )
    block_total = inclusive[:, :, -1, :]
    block_decay = jnp.exp(block_total)
    key_end = lookups_b * jnp.exp(block_total[:, :, None, :] - inclusive)
    block_kv = jnp.einsum("bhts,bhtj->bhsj", key_end, values_b, precision=EXACT_ARITHMETIC)
    sweep = jnp.zeros((attenders_on_shard, ATTENTION_DEPTH, ATTENTION_DEPTH), jnp.float32)
    factor = jnp.ones((attenders_on_shard, ATTENTION_DEPTH), jnp.float32)
    starts, factors_before, ends, factors_after = ([], [], [], [])
    for number in range(blocks):
        sweep = sweep * keep_state[number]
        factor = factor * keep_factor[number]
        starts.append(sweep)
        factors_before.append(factor)
        sweep = block_decay[number][:, :, None] * sweep + block_kv[number]
        factor = factor * block_decay[number]
        ends.append(sweep)
        factors_after.append(factor)
    block_out = intra + jnp.einsum(
        "bhts,bhsj->bhtj", query_scaled, jnp.stack(starts), precision=EXACT_ARITHMETIC
    )
    carry_rows = query_scaled * jnp.stack(factors_before)[:, :, None, :]
    block_states = jnp.stack(ends)
    block_factors = jnp.stack(factors_after)
    page_end = block_states[per_page - 1 :: per_page]
    page_factor = block_factors[per_page - 1 :: per_page]
    last_pick = (slot_number == live_count - 1).astype(jnp.float32)
    leaving_state = jnp.einsum("s,shij->hij", last_pick, page_end, precision=EXACT_ARITHMETIC)
    leaving_factor = jnp.einsum("s,shi->hi", last_pick, page_factor, precision=EXACT_ARITHMETIC)
    leaving_pack = jnp.concatenate([leaving_state, leaving_factor[:, None, :]], axis=1)
    every_pack = lax.all_gather(leaving_pack, "group", axis=0, tiled=False)
    incoming = jnp.zeros_like(leaving_state)
    for number in range(group_count - 1):
        composed = (
            every_pack[number, :, ATTENTION_DEPTH, :][:, :, None] * incoming
            + every_pack[number, :, :ATTENTION_DEPTH, :]
        )
        incoming = jnp.where(number < group_here, composed, incoming)
    block_out = block_out + jnp.einsum(
        "bhts,hsj->bhtj", carry_rows, incoming, precision=EXACT_ARITHMETIC
    )
    page_end = page_end + page_factor[:, :, :, None] * incoming[None]
    attended = block_out.transpose(0, 2, 1, 3).reshape(slot_rows, features_on_shard)
    normed = (group_norm(attended) * attender_scaling_coefs * gating).astype(jnp.bfloat16)
    mixer_total = lax.psum(
        lax.dot_general(
            normed, output_weight_t, (((1,), (1,)), ((), ())), preferred_element_type=jnp.float32
        ).astype(jnp.bfloat16),
        "head",
    ).astype(jnp.float32)
    residual = (embedded.astype(jnp.float32) + mixer_total).astype(jnp.bfloat16)
    last_residual = lax.dynamic_slice_in_dim(residual, live_count * PAGE - 1, 1, 0)
    arriving = passed_along(last_residual, "group", 1)
    channel_in = layer_norm(residual)
    channel_pages = channel_in.reshape(SLOTS, PAGE, full_width)
    edge_two = (
        jnp.concatenate([layer_norm(arriving), channel_pages[:-1, -1, :]], axis=0)
        * continues[:, None]
    )
    channel_prev = jnp.concatenate(
        [edge_two[:, None, :], channel_pages[:, :-1, :]], axis=1
    ).reshape(slot_rows, full_width)
    channel_delta = channel_prev - channel_in
    key_input = (channel_in + channel_delta * lag_blend_coefs[6]).astype(jnp.bfloat16)
    gate_input = (channel_in + channel_delta * lag_blend_coefs[7]).astype(jnp.bfloat16)
    gate_raw_two = jnp.dot(gate_input, projections[4], preferred_element_type=jnp.float32)
    key_raw = jnp.dot(key_input, key_weight, preferred_element_type=jnp.float32)
    squared = jnp.square(jax.nn.relu(key_raw)).astype(jnp.bfloat16)
    channel = lax.psum_scatter(
        lax.dot_general(
            squared, value_weight_t, (((1,), (1,)), ((), ())), preferred_element_type=jnp.float32
        ).astype(jnp.bfloat16),
        "head",
        scatter_dimension=1,
        tiled=True,
    ).astype(jnp.float32)
    gate_two = jax.nn.sigmoid(gate_raw_two)
    residual_local = lax.dynamic_slice_in_dim(
        residual, head_here * features_on_shard, features_on_shard, 1
    )
    hidden = (residual_local.astype(jnp.float32) + gate_two * channel).astype(jnp.bfloat16)
    row_live = jnp.repeat(slot_live, PAGE)
    hidden_out = jnp.where(row_live[:, None], hidden, jnp.zeros_like(hidden))
    state_out = page_end.reshape(SLOTS, attenders_on_shard, ATTENTION_DEPTH * ATTENTION_DEPTH)
    state_out = jnp.where(slot_live[:, None, None], state_out, jnp.zeros_like(state_out))
    first_edge = lax.dynamic_slice_in_dim(
        current_pages[:, -1, :], head_here * features_on_shard, features_on_shard, 1
    )
    second_edge = lax.dynamic_slice_in_dim(
        channel_pages[:, -1, :], head_here * features_on_shard, features_on_shard, 1
    )
    edge_out = jnp.stack([first_edge, second_edge], axis=1)
    edge_out = jnp.where(slot_live[:, None, None], edge_out, jnp.zeros_like(edge_out))
    return (hidden_out, state_out, edge_out)


def solution(mesh):
    in_specs = (
        P(None, "head"),
        P(None, "group", "head"),
        P("group", "head"),
        P("head", "group"),
        P("head", "group"),
        P(),
        P(),
        P(),
        P(),
        P(None, "head"),
        P("head"),
        P("head"),
        P("head"),
        P(),
        P(),
        P(),
    )
    out_specs = (P("group", "head"), P("group", "head", None), P("group", None, "head"))
    return jax.shard_map(
        per_device, mesh=mesh, in_specs=in_specs, out_specs=out_specs, check_vma=False
    )
```

profile of v0, /device:TPU:0, one launch (start us, length us, event | category | flops | bytes accessed | tf_op | source)
XLA Modules:
  0.0 557.0 jit_solution(13444309957814497587)
XLA Ops:
  20.8 10.5 %gather_fusion.2 = bf16[1032,128]{1,0:T(8,128)(2,1)S(1)} fusion(bf16[65536,128]{1,0:T(8,128)(2,1)} %param.18, s32[2048]{0:T(1024)S(1)} %pad_clamp_fusion), kind=kCustom, calls=%fused_computation.4 | custom fusion | bytes 532512 | tf_op jit(solution)/shard_map/jit(_take)/gather | solution.py:104
  43.5 13.4 %all-gather.7.cloned.1.call-done = bf16[6,2048,128]{2,1,0:T(8,128)(2,1)} async-done(((bf16[6,256,128]{2,1,0:T(8,128)(2,1)}), bf16[6,2048,128]{2,1,0:T(8,128)(2,1)}) %all-gather.7.cloned.1.call-update) | async-done | bytes 3145744 | tf_op jit(solution)/shard_map/all_gather | solution.py:115
  61.4 54.3 %all-gather.5.cloned.1.call-done = bf16[1032,2048]{1,0:T(8,128)(2,1)} async-done(((bf16[1032,128]{1,0:T(8,128)(2,1)}), bf16[1032,2048]{1,0:T(8,128)(2,1)}) %all-gather.5.cloned.1.call-update) | async-done | bytes 4227088 | tf_op jit(solution)/shard_map/all_gather | solution.py:105
  125.3 4.7 pad_maximum_fusion
  131.0 4.2 bitcast_subtract_fusion.1
  138.4 8.1 %fusion.29 = bf16[1024,64]{0,1:T(8,128)(2,1)S(1)} fusion(bf16[2048,64]{0,1:T(8,128)(2,1)S(1)} %copy-done.18, f32[1024,2048]{1,0:T(8,128)} %copy-done.2, f32[2048]{0:T(1024)S(1)} %bitcast.330, f32[1024]{0:T(1024)S(1)} %add_rsqrt_fusion.1, f32[1024]{0:T(1024)S(1)} %broadcast_multiply_fusion.2, bf16[5,32,2048]{2,1,0:T(8,128)(2,1)} %param.25, ...), kind=kOutput, calls=%fused_computation.63 | convolution fusion | flops 417398784 | bytes 13189120 | tf_op jit(solution)/shard_map/dot_general | solution.py:48
  149.2 5.0 slice_multiply_fusion.2
  155.0 6.8 %add_convert_fusion.3 = bf16[1024,2048]{1,0:T(8,128)(2,1)S(1)} fusion(f32[1024,2048]{1,0:T(8,128)} %copy-done.2, f32[2048]{0:T(1024)S(1)} %bitcast.323, f32[1024]{0:T(1024)S(1)} %add_rsqrt_fusion.1, f32[1024]{0:T(1024)S(1)} %broadcast_multiply_fusion.2, bf16[5,32,2048]{2,1,0:T(8,128)(2,1)} %param.25, bf16[1024,160]{0,1:T(8,128)(2,1)} %copy-done.15, ...), kind=kOutput, calls=%fused_computation.24 | convolution fusion | flops 148897792 | bytes 16990208 | tf_op jit(solution)/shard_map/dot_general | solution.py:37
  163.4 7.5 %add_convert_fusion.6 = bf16[1024,2048]{1,0:T(8,128)(2,1)S(1)} fusion(f32[1024,2048]{1,0:T(8,128)} %copy-done.2, f32[2048]{0:T(1024)S(1)} %bitcast.322, f32[1024]{0:T(1024)S(1)} %add_rsqrt_fusion.1, f32[1024]{0:T(1024)S(1)} %broadcast_multiply_fusion.2, bf16[5,32,2048]{2,1,0:T(8,128)(2,1)} %param.25, bf16[1024,160]{0,1:T(8,128)(2,1)} %copy-done.15, ...), kind=kOutput, calls=%fused_computation.27 | convolution fusion | flops 148897792 | bytes 16990208 | tf_op jit(solution)/shard_map/dot_general | solution.py:37
  172.5 3.3 add_convert_fusion.4
  187.9 29.0 %all-gather = f32[16,65,64]{1,2,0:T(8,128)S(1)} all-gather(f32[2,65,64]{1,2,0:T(8,128)S(1)} %pad_maximum_fusion.4), channel_id=2, replica_groups=mesh['group'=8,'head'=16] {'group'}, dimensions={0}, use_global_device_ids=true | all-gather | bytes 299520 | tf_op jit(solution)/shard_map/all_gather | solution.py:197
  222.0 7.5 %multiply_convert_fusion.1 = bf16[1024,128]{1,0:T(8,128)(2,1)S(1)} fusion(bf16[6,2048,128]{2,1,0:T(8,128)(2,1)} %all-gather.7.cloned.1.call-done, f32[1024,2048]{1,0:T(8,128)} %copy-done.2, f32[2048]{0:T(1024)S(1)} %bitcast.329, f32[1024]{0:T(1024)S(1)} %add_rsqrt_fusion.1, f32[1024]{0:T(1024)S(1)} %broadcast_multiply_fusion.2, f32[1024,128]{1,0:T(8,128)S(1)} %copy.137, ...), kind=kOutput, calls=%fused_computation.81 | convolution fusion | flops 686948352 | bytes 15155712 | tf_op jit(solution)/shard_map/dot_general | solution.py:136
  229.5 4.3 convolution_convert_fusion.1
  235.6 146.8 %all-reduce.2.cloned.1.call-done = bf16[1024,2048]{1,0:T(8,128)(2,1)} async-done(((bf16[1024,2048]{1,0:T(8,128)(2,1)}), bf16[1024,2048]{1,0:T(8,128)(2,1)}) %all-reduce.2.cloned.1.call-update) | async-done | bytes 4194320 | tf_op jit(solution)/shard_map/psum | solution.py:211
  382.4 4.2 convert_reduce_fusion.1
  386.6 3.5 collective-permute-start
  392.3 3.2 copy-done.5
  398.3 4.6 pad_maximum_fusion.1
  402.9 4.5 bitcast_subtract_fusion
  407.4 33.2 %all-gather.9.cloned.1.call-done = bf16[2,2048,448]{1,2,0:T(8,128)(2,1)} async-done(((bf16[2,256,448]{1,2,0:T(8,128)(2,1)}), bf16[2,2048,448]{1,2,0:T(8,128)(2,1)}) %all-gather.9.cloned.1.call-update) | async-done | bytes 3670032 | tf_op jit(solution)/shard_map/all_gather | solution.py:116
  440.6 12.2 %convolution_convert_fusion = bf16[1024,2048]{1,0:T(8,128)(2,1)} fusion(bf16[2,2048,448]{1,2,0:T(8,128)(2,1)} %all-gather.9.cloned.1.call-done, f32[1024,2048]{1,0:T(8,128)} %bitcast_subtract_fusion, f32[2048]{0:T(1024)S(1)} %bitcast.328, bf16[1024,2048]{1,0:T(8,128)(2,1)} %copy-done.3, f32[1024]{0:T(1024)S(1)} %add_rsqrt_fusion, ...), kind=kOutput, calls=%fused_computation.34 | convolution fusion | flops 3774152704 | bytes 20463616 | tf_op jit(solution)/shard_map/dot_general | solution.py:236
  452.8 6.5 %copy.152 = bf16[1024,2048]{0,1:T(8,128)(2,1)} copy(bf16[1024,2048]{1,0:T(8,128)(2,1)} %convolution_convert_fusion) | data formatting | bytes 8388608
  464.0 77.8 %reduce-scatter.4.cloned.1.call-done = bf16[128,1024]{1,0:T(8,128)(2,1)} async-done(((bf16[2048,1024]{1,0:T(8,128)(2,1)}), bf16[128,1024]{1,0:T(8,128)(2,1)}) %reduce-scatter.4.cloned.1.call-update) | async-done | bytes 262160
  543.0 7.3 %fusion.30 = bf16[1024,128]{1,0:T(8,128)(2,1)} fusion(f32[1024,2048]{1,0:T(8,128)} %bitcast_subtract_fusion, f32[2048]{0:T(1024)S(1)} %bitcast.327, bf16[6,2048,128]{2,1,0:T(8,128)(2,1)} %all-gather.7.cloned.1.call-done, bf16[1024,128]{1,0:T(8,128)(2,1)S(1)} %copy.153, bf16[1024,2048]{1,0:T(8,128)(2,1)} %copy-done.3, s32[]{:T(128)S(6)} %select_n.286, ...), kind=kOutput, calls=%fused_computation.65 | convolution fusion | flops 550633472 | bytes 13911044 | tf_op jit(solution)/shard_map/dot_general | solution.py:232
  (196 shorter events, 76.4 us)
Async XLA Ops:
  7.2 128.0 %copy-start = (bf16[2048,160]{0,1:T(8,128)(2,1)S(1)}, bf16[2048,160]{0,1:T(8,128)(2,1)}, u32[]{:S(2)}) copy-start(bf16[2048,160]{0,1:T(8,128)(2,1)} %param.24) | copy-start | bytes 1966084
  7.2 49.7 %all-gather.7.cloned.1.call-start = ((), (), s32[]{:S(2)}) async-start(), calls=%async_computation.2 | async-start | bytes 3538944 | tf_op jit(solution)/shard_map/all_gather | solution.py:115
  10.3 105.4 %all-gather.5.cloned.1.call-start = ((), (), s32[]{:S(2)}) async-start(), calls=%async_computation.1 | async-start | bytes 4491264 | tf_op jit(solution)/shard_map/all_gather | solution.py:105
  33.6 348.7 %all-reduce.2.cloned.1.call-start = ((), (), s32[]{:S(2)}) async-start(), calls=%async_computation.3 | async-start | bytes 8388608 | tf_op jit(solution)/shard_map/psum | solution.py:211
  115.7 8.2 %slice-start = ((s8[4227072]{0:T(1024)(128)(4,1)}), s8[4194304]{0:T(1024)(128)(4,1)S(1)}, s32[]{:S(2)}) async-start(s8[4227072]{0:T(1024)(128)(4,1)} %bitcast.296), calls=%async_computation.6 | async-start | bytes 8388608
  118.0 5.9 %slice-start.1 = ((s8[4227072]{0:T(1024)(128)(4,1)}), s8[32768]{0:T(1024)(128)(4,1)S(1)}, s32[]{:S(2)}) async-start(s8[4227072]{0:T(1024)(128)(4,1)} %bitcast.296), calls=%async_computation.7 | async-start | bytes 65536
  125.2 5.7 %copy-start.6 = (f32[1024,2048]{1,0:T(8,128)}, f32[1024,2048]{1,0:T(8,128)S(1)}, u32[]{:S(2)}) copy-start(f32[1024,2048]{1,0:T(8,128)S(1)} %fusion.2) | copy-start | bytes 25165828
  138.4 8.1 %copy-start.15 = (bf16[1024,160]{0,1:T(8,128)(2,1)}, bf16[1024,160]{0,1:T(8,128)(2,1)S(1)}, u32[]{:S(2)}) copy-start(bf16[1024,160]{0,1:T(8,128)(2,1)S(1)} %fusion.22) | copy-start | bytes 983044
  138.4 8.1 %copy-start.16 = (bf16[64,128]{1,0:T(8,128)(2,1)S(1)}, bf16[64,128]{1,0:T(8,128)(2,1)}, u32[]{:S(2)}) copy-start(bf16[64,128]{1,0:T(8,128)(2,1)} %param.27) | copy-start | bytes 49156
  138.4 8.1 %copy-start.17 = (f32[128]{0:T(128)S(1)}, f32[128]{0:T(128)}, u32[]{:S(2)}) copy-start(f32[128]{0:T(128)} %param.28) | copy-start | bytes 1540
  155.0 6.8 %copy-start.9 = (bf16[128,2048]{1,0:T(8,128)(2,1)S(1)}, bf16[128,2048]{1,0:T(8,128)(2,1)}, u32[]{:S(2)}) copy-start(bf16[128,2048]{1,0:T(8,128)(2,1)} %copy.128) | copy-start | bytes 1572868
  161.8 10.7 %slice-start.2 = ((s8[4227072]{0:T(1024)(128)(4,1)}), s8[4194304]{0:T(1024)(128)(4,1)S(1)}, s32[]{:S(2)}) async-start(s8[4227072]{0:T(1024)(128)(4,1)} %bitcast.298), calls=%async_computation.8 | async-start | bytes 8388608
  161.8 10.7 %slice-start.4 = ((s8[8388608]{0:T(1024)(128)(4,1)}), s8[4194304]{0:T(1024)(128)(4,1)S(1)}, s32[]{:S(2)}) async-start(s8[8388608]{0:T(1024)(128)(4,1)} %bitcast.300), calls=%async_computation.10 | async-start | bytes 8388608
  163.4 7.6 %copy-start.8 = (bf16[128,2048]{1,0:T(8,128)(2,1)S(1)}, bf16[128,2048]{1,0:T(8,128)(2,1)}, u32[]{:S(2)}) copy-start(bf16[128,2048]{1,0:T(8,128)(2,1)} %copy.121) | copy-start | bytes 1572868
  163.4 9.1 %slice-start.3 = ((s8[4227072]{0:T(1024)(128)(4,1)}), s8[32768]{0:T(1024)(128)(4,1)S(1)}, s32[]{:S(2)}) async-start(s8[4227072]{0:T(1024)(128)(4,1)} %bitcast.298), calls=%async_computation.9 | async-start | bytes 65536
  163.4 9.1 %slice-start.5 = ((s8[8388608]{0:T(1024)(128)(4,1)}), s8[4194304]{0:T(1024)(128)(4,1)S(1)}, s32[]{:S(2)}) async-start(s8[8388608]{0:T(1024)(128)(4,1)} %bitcast.300), calls=%async_computation.11 | async-start | bytes 8388608
  175.8 4.9 copy-start.12
  182.3 39.8 %copy-start.19 = (f32[128]{0:T(128)S(1)}, f32[128]{0:T(128)}, u32[]{:S(2)}) copy-start(f32[128]{0:T(128)} %param.30) | copy-start | bytes 1540
  233.9 206.7 %all-gather.9.cloned.1.call-start = ((), (), s32[]{:S(2)}) async-start(), calls=%async_computation.4 | async-start | bytes 4128768 | tf_op jit(solution)/shard_map/all_gather | solution.py:116
  234.9 306.9 %reduce-scatter.4.cloned.1.call-start = ((), (), s32[]{:S(2)}) async-start(), calls=%async_computation.5 | async-start | bytes 4456448
  386.5 5.8 %copy-start.3 = (bf16[1024,2048]{1,0:T(8,128)(2,1)}, bf16[1024,2048]{1,0:T(8,128)(2,1)S(1)}, u32[]{:S(2)}) copy-start(bf16[1024,2048]{1,0:T(8,128)(2,1)S(1)} %get-tuple-element.14) | copy-start | bytes 12582916
  386.6 9.0 %collective-permute-start = (bf16[1,2048]{1,0:T(2,128)(2,1)S(1)}, bf16[1,2048]{1,0:T(2,128)(2,1)S(1)}, u32[]{:S(2)}, u32[]{:S(2)}) collective-permute-start(bf16[1,2048]{1,0:T(2,128)(2,1)S(1)} %constant_dynamic-slice_fusion.2), channel_id=1, source_target_pairs={{0,16},{16,32},{32,48},{48,64},{64,80},{80,96},{96,112},{1,17},{17... | collective-permute-start | bytes 12296 | tf_op jit(solution)/shard_map/ppermute | solution.py:18
  452.8 8.4 %copy-start.11 = (f32[7,2,64,64]{3,2,1,0:T(8,128)S(1)}, f32[7,2,64,64]{3,2,1,0:T(8,128)}, u32[]{:S(2)}) copy-start(f32[7,2,64,64]{3,2,1,0:T(8,128)} %copy-done.10) | copy-start | bytes 688132
  541.8 8.5 %copy-start.1 = (bf16[2048,160]{0,1:T(8,128)(2,1)S(1)}, bf16[2048,160]{0,1:T(8,128)(2,1)}, u32[]{:S(2)}) copy-start(bf16[2048,160]{0,1:T(8,128)(2,1)} %param.24) | copy-start | bytes 1966084
  (8 other events, 27.5 us)
Sparse Core Ops, SparseCore 0:
  10.4 46.4 all-gather.6
  59.2 56.5 all-gather.4
  234.0 148.2 all-reduce.1
  383.8 56.7 all-gather.8
  459.4 82.2 reduce-scatter.3
where the time goes:
time: 561 us; the launch traced here: 557 us
  waiting for transfers between devices  326 us (58%)
  matrix products  72.5 us (13%)
  other arithmetic  65.3 us (12%)
  local copies, waits for them, and re-layouts  42.4 us (8%)
  blocking collectives  29 us (5%)
  between operations  18.2 us (3%)
    psum x1, waiting for transfers between devices, per_device(): lax.psum(lax.dot_general(normed, output_weight_t, (((1,), (1,)), ((), ())...  147 us
    unnamed x6, waiting for transfers between devices  77.9 us
    all_gather x1, waiting for transfers between devices, per_device(): gathered_rows = lax.all_gather(own_rows, 'head', axis=1, tiled=True)  54.3 us
    all_gather x1, waiting for transfers between devices, per_device(): second_full = lax.all_gather(second_pack, 'group', axis=1, tiled=True)  33.2 us
    all_gather x1, blocking collectives, per_device(): every_pack = lax.all_gather(leaving_pack, 'group', axis=0, tiled=False)  29 us
    dot_general x3, matrix products, mixed_inputs(): jnp.dot(column_part, blend_widening_maps[number], preferred_element_type=...  17.6 us
    all_gather x1, waiting for transfers between devices, per_device(): first_full = lax.all_gather(first_pack, 'group', axis=1, tiled=True)  13.4 us
    unnamed x57, local copies, waits for them, and re-layouts  13.2 us
  transfers between devices with their start and end apart: 6, of which 5 were waited for; matrix products, arithmetic and copies ran while one was open for 10% of the time, Pallas kernels for 0%

commit v1 on v0

--- a/solution.py
+++ b/solution.py
@@ -208,11 +208,17 @@
     page_end = page_end + page_factor[:, :, :, None] * incoming[None]
     attended = block_out.transpose(0, 2, 1, 3).reshape(slot_rows, features_on_shard)
     normed = (group_norm(attended) * attender_scaling_coefs * gating).astype(jnp.bfloat16)
-    mixer_total = lax.psum(
-        lax.dot_general(
-            normed, output_weight_t, (((1,), (1,)), ((), ())), preferred_element_type=jnp.float32
-        ).astype(jnp.bfloat16),
-        "head",
+    mixer_total = jnp.sum(
+        lax.all_gather(
+            lax.dot_general(
+                normed,
+                output_weight_t,
+                (((1,), (1,)), ((), ())),
+                preferred_element_type=jnp.float32,
+            ).astype(jnp.bfloat16),
+            axis_name="head",
+        ),
+        axis=0,
     ).astype(jnp.float32)
     residual = (embedded.astype(jnp.float32) + mixer_total).astype(jnp.bfloat16)
     last_residual = lax.dynamic_slice_in_dim(residual, live_count * PAGE - 1, 1, 0)

time: 561 us -> 746 us (1.33)
  waiting for transfers between devices: 326 us -> 486 us
  other arithmetic: 65.3 us -> 89.8 us
    all_gather x0 -> x1, waiting for transfers between devices: none -> 335 us  [per_device(): lax.all_gather(lax.dot_general(normed, output_weight_t, (((1,), (1,)), ((...]
    psum x1 -> x0, waiting for transfers between devices: 147 us -> none  [per_device(): lax.psum(lax.dot_general(normed, output_weight_t, (((1,), (1,)), ((), ())...]
    all_gather x1, waiting for transfers between devices: 33.2 us -> 5.66 us  [per_device(): second_full = lax.all_gather(second_pack, 'group', axis=1, tiled=True)]
    reduce_sum x0 -> x1, other arithmetic: none -> 24.2 us  [per_device(): jnp.sum(lax.all_gather(lax.dot_general(normed, output_weight_t, (((1,), (...]
  transfers between devices with their start and end apart: 6 -> 6, of which waited for: 5 -> 5; matrix products, arithmetic and copies ran while one was open for 10% -> 11% of each run, Pallas kernels for 0% -> 0%
where the time goes in v1:
time: 746 us; the launch traced here: 742 us
  waiting for transfers between devices  486 us (65%)
  other arithmetic  89.8 us (12%)
  matrix products  72.5 us (10%)
  local copies, waits for them, and re-layouts  42.4 us (6%)
  blocking collectives  29 us (4%)
  between operations  18.3 us (2%)
    all_gather x1, waiting for transfers between devices, per_device(): lax.all_gather(lax.dot_general(normed, output_weight_t, (((1,), (1,)), ((...  335 us
    unnamed x6, waiting for transfers between devices  77.4 us
    all_gather x1, waiting for transfers between devices, per_device(): gathered_rows = lax.all_gather(own_rows, 'head', axis=1, tiled=True)  54.3 us
    all_gather x1, blocking collectives, per_device(): every_pack = lax.all_gather(leaving_pack, 'group', axis=0, tiled=False)  29 us
    reduce_sum x1, other arithmetic, per_device(): jnp.sum(lax.all_gather(lax.dot_general(normed, output_weight_t, (((1,), (...  24.2 us
    dot_general x3, matrix products, mixed_inputs(): jnp.dot(column_part, blend_widening_maps[number], preferred_element_type=...  17.6 us
  transfers between devices with their start and end apart: 6, of which 5 were waited for; matrix products, arithmetic and copies ran while one was open for 11% of the time, Pallas kernels for 0%

profile of v1, /device:TPU:0, one launch (start us, length us, event | category | flops | bytes accessed | tf_op | source)
XLA Modules:
  0.0 741.6 jit_solution(4608810076472384271)
XLA Ops:
  20.8 10.5 %gather_fusion.2 = bf16[1032,128]{1,0:T(8,128)(2,1)S(1)} fusion(bf16[65536,128]{1,0:T(8,128)(2,1)} %param.18, s32[2048]{0:T(1024)S(1)} %pad_clamp_fusion), kind=kCustom, calls=%fused_computation.4 | custom fusion | bytes 532512 | tf_op jit(solution)/shard_map/jit(_take)/gather | solution.py:104
  43.6 13.3 %all-gather.9.cloned.1.call-done = bf16[6,2048,128]{2,1,0:T(8,128)(2,1)} async-done(((bf16[6,256,128]{2,1,0:T(8,128)(2,1)}), bf16[6,2048,128]{2,1,0:T(8,128)(2,1)}) %all-gather.9.cloned.1.call-update) | async-done | bytes 3145744 | tf_op jit(solution)/shard_map/all_gather | solution.py:115
  61.5 54.3 %all-gather.7.cloned.1.call-done = bf16[1032,2048]{1,0:T(8,128)(2,1)} async-done(((bf16[1032,128]{1,0:T(8,128)(2,1)}), bf16[1032,2048]{1,0:T(8,128)(2,1)}) %all-gather.7.cloned.1.call-update) | async-done | bytes 4227088 | tf_op jit(solution)/shard_map/all_gather | solution.py:105
  125.3 4.7 pad_maximum_fusion
  130.9 4.2 bitcast_subtract_fusion.1
  138.4 8.0 %fusion.29 = bf16[1024,64]{0,1:T(8,128)(2,1)S(1)} fusion(bf16[2048,64]{0,1:T(8,128)(2,1)S(1)} %copy-done.18, f32[1024,2048]{1,0:T(8,128)} %copy-done.2, f32[2048]{0:T(1024)S(1)} %bitcast.331, f32[1024]{0:T(1024)S(1)} %add_rsqrt_fusion.1, f32[1024]{0:T(1024)S(1)} %broadcast_multiply_fusion.2, bf16[5,32,2048]{2,1,0:T(8,128)(2,1)} %param.25, ...), kind=kOutput, calls=%fused_computation.63 | convolution fusion | flops 417398784 | bytes 13189120 | tf_op jit(solution)/shard_map/dot_general | solution.py:48
  149.2 5.1 slice_multiply_fusion.2
  155.1 6.8 add_convert_fusion.3
  163.5 7.6 %add_convert_fusion.6 = bf16[1024,2048]{1,0:T(8,128)(2,1)S(1)} fusion(f32[1024,2048]{1,0:T(8,128)} %copy-done.2, f32[2048]{0:T(1024)S(1)} %bitcast.323, f32[1024]{0:T(1024)S(1)} %add_rsqrt_fusion.1, f32[1024]{0:T(1024)S(1)} %broadcast_multiply_fusion.2, bf16[5,32,2048]{2,1,0:T(8,128)(2,1)} %param.25, bf16[1024,160]{0,1:T(8,128)(2,1)} %copy-done.15, ...), kind=kOutput, calls=%fused_computation.27 | convolution fusion | flops 148897792 | bytes 16990208 | tf_op jit(solution)/shard_map/dot_general | solution.py:37
  172.7 3.3 add_convert_fusion.4
  188.1 29.0 %all-gather = f32[16,65,64]{1,2,0:T(8,128)S(1)} all-gather(f32[2,65,64]{1,2,0:T(8,128)S(1)} %pad_maximum_fusion.4), channel_id=2, replica_groups=mesh['group'=8,'head'=16] {'group'}, dimensions={0}, use_global_device_ids=true | all-gather | bytes 299520 | tf_op jit(solution)/shard_map/all_gather | solution.py:197
  222.2 7.5 %multiply_convert_fusion.1 = bf16[1024,128]{1,0:T(8,128)(2,1)S(1)} fusion(bf16[6,2048,128]{2,1,0:T(8,128)(2,1)} %all-gather.9.cloned.1.call-done, f32[1024,2048]{1,0:T(8,128)} %copy-done.2, f32[2048]{0:T(1024)S(1)} %bitcast.330, f32[1024]{0:T(1024)S(1)} %add_rsqrt_fusion.1, f32[1024]{0:T(1024)S(1)} %broadcast_multiply_fusion.2, f32[1024,128]{1,0:T(8,128)S(1)} %copy.137, ...), kind=kOutput, calls=%fused_computation.81 | convolution fusion | flops 686948352 | bytes 15155712 | tf_op jit(solution)/shard_map/dot_general | solution.py:136
  229.7 4.4 convolution_convert_fusion.1
  235.8 335.1 %all-gather.13.cloned.1.call-done = bf16[16384,2048]{1,0:T(8,128)(2,1)} async-done(((bf16[1024,2048]{1,0:T(8,128)(2,1)}), bf16[16384,2048]{1,0:T(8,128)(2,1)}) %all-gather.13.cloned.1.call-update) | async-done | bytes 67108880 | tf_op jit(solution)/shard_map/all_gather | solution.py:212
  570.9 24.2 %reduce_sum.138 = bf16[1024,2048]{1,0:T(8,128)(2,1)} reduce(bf16[16,1024,2048]{2,1,0:T(8,128)(2,1)} %bitcast.100, bf16[]{:T(256)} %constant.167.clone.1), dimensions={0}, to_apply=%region_13.15 | reduce | flops 31457280 | bytes 71303168 | tf_op jit(solution)/shard_map/reduce_sum | solution.py:211
  595.1 4.2 convert_reduce_fusion.1
  599.4 3.4 collective-permute-start
  610.9 4.6 pad_maximum_fusion.1
  615.6 4.5 bitcast_subtract_fusion
  620.1 5.7 all-gather.11.cloned.1.call-done
  625.8 12.2 %convolution_convert_fusion = bf16[1024,2048]{1,0:T(8,128)(2,1)} fusion(bf16[2,2048,448]{1,2,0:T(8,128)(2,1)} %all-gather.11.cloned.1.call-done, f32[1024,2048]{1,0:T(8,128)} %bitcast_subtract_fusion, f32[2048]{0:T(1024)S(1)} %bitcast.329, bf16[1024,2048]{1,0:T(8,128)(2,1)} %copy-done.3, f32[1024]{0:T(1024)S(1)} %add_rsqrt_fusion, ...), kind=kOutput, calls=%fused_computation.34 | convolution fusion | flops 3774152704 | bytes 20463616 | tf_op jit(solution)/shard_map/dot_general | solution.py:242
  637.9 6.5 copy.152
  649.1 77.4 %reduce-scatter.4.cloned.1.call-done = bf16[128,1024]{1,0:T(8,128)(2,1)} async-done(((bf16[2048,1024]{1,0:T(8,128)(2,1)}), bf16[128,1024]{1,0:T(8,128)(2,1)}) %reduce-scatter.4.cloned.1.call-update) | async-done | bytes 262160
  727.6 7.3 fusion.30
  (197 shorter events, 79.6 us)
Async XLA Ops:
  7.2 128.0 %copy-start = (bf16[2048,160]{0,1:T(8,128)(2,1)S(1)}, bf16[2048,160]{0,1:T(8,128)(2,1)}, u32[]{:S(2)}) copy-start(bf16[2048,160]{0,1:T(8,128)(2,1)} %param.24) | copy-start | bytes 1966084
  7.2 49.7 %all-gather.9.cloned.1.call-start = ((), (), s32[]{:S(2)}) async-start(), calls=%async_computation.2 | async-start | bytes 3538944 | tf_op jit(solution)/shard_map/all_gather | solution.py:115
  10.3 105.4 %all-gather.7.cloned.1.call-start = ((), (), s32[]{:S(2)}) async-start(), calls=%async_computation.1 | async-start | bytes 4491264 | tf_op jit(solution)/shard_map/all_gather | solution.py:105
  33.7 537.2 %all-gather.13.cloned.1.call-start = ((), (), s32[]{:S(2)}) async-start(), calls=%async_computation.4 | async-start | bytes 71303168 | tf_op jit(solution)/shard_map/all_gather | solution.py:212
  115.7 8.2 %slice-start = ((s8[4227072]{0:T(1024)(128)(4,1)}), s8[4194304]{0:T(1024)(128)(4,1)S(1)}, s32[]{:S(2)}) async-start(s8[4227072]{0:T(1024)(128)(4,1)} %bitcast.297), calls=%async_computation.6 | async-start | bytes 8388608
  118.0 5.9 slice-start.1
  125.3 5.7 copy-start.6
  138.4 8.1 %copy-start.15 = (bf16[1024,160]{0,1:T(8,128)(2,1)}, bf16[1024,160]{0,1:T(8,128)(2,1)S(1)}, u32[]{:S(2)}) copy-start(bf16[1024,160]{0,1:T(8,128)(2,1)S(1)} %fusion.22) | copy-start | bytes 983044
  138.4 8.1 %copy-start.16 = (bf16[64,128]{1,0:T(8,128)(2,1)S(1)}, bf16[64,128]{1,0:T(8,128)(2,1)}, u32[]{:S(2)}) copy-start(bf16[64,128]{1,0:T(8,128)(2,1)} %param.27) | copy-start | bytes 49156
  138.4 8.1 %copy-start.17 = (f32[128]{0:T(128)S(1)}, f32[128]{0:T(128)}, u32[]{:S(2)}) copy-start(f32[128]{0:T(128)} %param.28) | copy-start | bytes 1540
  155.1 6.8 copy-start.9
  162.0 10.7 %slice-start.2 = ((s8[4227072]{0:T(1024)(128)(4,1)}), s8[4194304]{0:T(1024)(128)(4,1)S(1)}, s32[]{:S(2)}) async-start(s8[4227072]{0:T(1024)(128)(4,1)} %bitcast.299), calls=%async_computation.8 | async-start | bytes 8388608
  162.0 10.7 %slice-start.4 = ((s8[8388608]{0:T(1024)(128)(4,1)}), s8[4194304]{0:T(1024)(128)(4,1)S(1)}, s32[]{:S(2)}) async-start(s8[8388608]{0:T(1024)(128)(4,1)} %bitcast.301), calls=%async_computation.10 | async-start | bytes 8388608
  163.5 7.6 %copy-start.8 = (bf16[128,2048]{1,0:T(8,128)(2,1)S(1)}, bf16[128,2048]{1,0:T(8,128)(2,1)}, u32[]{:S(2)}) copy-start(bf16[128,2048]{1,0:T(8,128)(2,1)} %copy.121) | copy-start | bytes 1572868
  163.5 9.1 %slice-start.3 = ((s8[4227072]{0:T(1024)(128)(4,1)}), s8[32768]{0:T(1024)(128)(4,1)S(1)}, s32[]{:S(2)}) async-start(s8[4227072]{0:T(1024)(128)(4,1)} %bitcast.299), calls=%async_computation.9 | async-start | bytes 65536
  163.5 9.1 %slice-start.5 = ((s8[8388608]{0:T(1024)(128)(4,1)}), s8[4194304]{0:T(1024)(128)(4,1)S(1)}, s32[]{:S(2)}) async-start(s8[8388608]{0:T(1024)(128)(4,1)} %bitcast.301), calls=%async_computation.11 | async-start | bytes 8388608
  176.0 4.9 copy-start.12
  182.4 39.9 %copy-start.19 = (f32[128]{0:T(128)S(1)}, f32[128]{0:T(128)}, u32[]{:S(2)}) copy-start(f32[128]{0:T(128)} %param.30) | copy-start | bytes 1540
  234.1 391.7 %all-gather.11.cloned.1.call-start = ((), (), s32[]{:S(2)}) async-start(), calls=%async_computation.3 | async-start | bytes 4128768 | tf_op jit(solution)/shard_map/all_gather | solution.py:116
  235.1 491.3 %reduce-scatter.4.cloned.1.call-start = ((), (), s32[]{:S(2)}) async-start(), calls=%async_computation.5 | async-start | bytes 4456448
  599.3 5.6 copy-start.3
  599.4 8.8 %collective-permute-start = (bf16[1,2048]{1,0:T(2,128)(2,1)S(1)}, bf16[1,2048]{1,0:T(2,128)(2,1)S(1)}, u32[]{:S(2)}, u32[]{:S(2)}) collective-permute-start(bf16[1,2048]{1,0:T(2,128)(2,1)S(1)} %constant_dynamic-slice_fusion.2), channel_id=1, source_target_pairs={{0,16},{16,32},{32,48},{48,64},{64,80},{80,96},{96,112},{1,17},{17... | collective-permute-start | bytes 12296 | tf_op jit(solution)/shard_map/ppermute | solution.py:18
  637.9 8.4 %copy-start.11 = (f32[7,2,64,64]{3,2,1,0:T(8,128)S(1)}, f32[7,2,64,64]{3,2,1,0:T(8,128)}, u32[]{:S(2)}) copy-start(f32[7,2,64,64]{3,2,1,0:T(8,128)} %copy-done.10) | copy-start | bytes 688132
  726.4 8.5 %copy-start.1 = (bf16[2048,160]{0,1:T(8,128)(2,1)S(1)}, bf16[2048,160]{0,1:T(8,128)(2,1)}, u32[]{:S(2)}) copy-start(bf16[2048,160]{0,1:T(8,128)(2,1)} %param.24) | copy-start | bytes 1966084
  (8 other events, 27.6 us)
Sparse Core Ops, SparseCore 0:
  10.4 46.4 all-gather.8
  59.2 56.4 all-gather.6
  234.2 336.6 all-gather.12
  572.3 53.3 all-gather.10
  644.5 81.8 reduce-scatter.3
